TPU v7x, 32 devices: a whole 2x2x4 slice. The times are simulated.
32 devices in a mesh: dp: 2 (over y), seq: 16 (over z, x, core).
Axes of the slice: x: 2, y: 2, z: 4, core: 2. Of those that a mesh axis runs over, the one named last changes fastest.
Arguments:
- inputs: bfloat16 [2, 256, 512, 512], P('dp', 'seq'), may hold values from -6 to 6
- gate_logits: bfloat16 [2, 256, 512, 512], P('dp', 'seq'), may hold values from -8 to 8
- kernel: bfloat16 [256, 512, 512], P(None, 'seq'), may hold values from -1.5 to 1.5
- cotangent: bfloat16 [2, 256, 512, 512], P('dp', 'seq'), may hold values from -6 to 6
- block_one: bfloat16 [256, 512, 512], P('seq'), may hold values from -0.25 to 0.25
- block_two: bfloat16 [512, 256, 256], P('seq'), may hold values from -0.375 to 0.375
Outputs:
- output: bfloat16 [2, 256, 512, 512], P('dp', 'seq')
- grad_inputs: bfloat16 [2, 256, 512, 512], P('dp', 'seq')
- grad_gate: bfloat16 [2, 256, 512, 512], P('dp', 'seq')
- grad_kernel: bfloat16 [256, 512, 512], P(None, 'seq', 'dp')
- grad_block_one: bfloat16 [256, 512, 512], P('seq', None, 'dp')
- grad_block_two: bfloat16 [512, 256, 256], P('seq', None, 'dp')
All inputs are finite; a program needn't handle non-finite values.
Results may differ from a plain program's by a relative error of at most 0.009.
Values may be sent and summed in bfloat16 or wider, within the bound.
No kernel may reach another device: no remote copies, remote signals or barrier semaphores. Data moves between devices by JAX's collectives and lax.ppermute only.
A program may use at most 320 MiB of HBM per device.

v0:
```python
import jax
import jax.numpy as jnp
from jax import lax
from jax.sharding import PartitionSpec as P


def body(inputs, gate_logits, kernel, cotangent, block_one, block_two):
    tokens = inputs[0]
    kernel_wide = kernel.astype(jnp.float32)
    grad_scale = (lax.axis_size("dp") * tokens.shape[2]) ** (-0.5)
    first = jnp.einsum(
        "acb,abd->acd", block_one, tokens, preferred_element_type=jnp.float32
    ).astype(jnp.bfloat16)
    arrived = lax.all_to_all(first, "seq", split_axis=1, concat_axis=0, tiled=True)
    first_cols = arrived
    second = jnp.einsum("cea,acd->ecd", block_two, arrived, preferred_element_type=jnp.float32)
    filtered = (kernel_wide * second).astype(jnp.bfloat16)
    third = jnp.einsum(
        "cef,ecd->fcd", block_two, filtered, preferred_element_type=jnp.float32
    ).astype(jnp.bfloat16)
    arrived = lax.all_to_all(third, "seq", split_axis=0, concat_axis=1, tiled=True)
    third_rows = arrived
    fourth = jnp.einsum(
        "fch,fcd->fhd", block_one, arrived, preferred_element_type=jnp.float32
    ).astype(jnp.bfloat16)
    opened = jax.nn.sigmoid(gate_logits[0].astype(jnp.float32))
    incoming = cotangent[0].astype(jnp.float32)
    fourth_wide = fourth.astype(jnp.float32)
    output = (opened * fourth_wide).astype(jnp.bfloat16)
    grad_gate = (incoming * fourth_wide * opened * (1.0 - opened)).astype(jnp.bfloat16)
    grad_fourth = (incoming * opened).astype(jnp.bfloat16)
    outer_one = jnp.einsum(
        "fhd,fcd->fch", grad_fourth, third_rows, preferred_element_type=jnp.float32
    )
    grad_third = jnp.einsum(
        "fch,fhd->fcd", block_one, grad_fourth, preferred_element_type=jnp.float32
    ).astype(jnp.bfloat16)
    arrived = lax.all_to_all(grad_third, "seq", split_axis=1, concat_axis=0, tiled=True)
    grad_third_cols = arrived
    grad_filtered = jnp.einsum(
        "cef,fcd->ecd", block_two, arrived, preferred_element_type=jnp.float32
    )
    outer_two = jnp.einsum(
        "fcd,ecd->cef", grad_third_cols, filtered, preferred_element_type=jnp.float32
    )
    grad_kernel = grad_filtered * second
    grad_second = (kernel_wide * grad_filtered).astype(jnp.bfloat16)
    grad_block_two = (
        outer_two
        + jnp.einsum("ecd,acd->cea", grad_second, first_cols, preferred_element_type=jnp.float32)
    ) * grad_scale
    grad_first = jnp.einsum(
        "cea,ecd->acd", block_two, grad_second, preferred_element_type=jnp.float32
    ).astype(jnp.bfloat16)
    arrived = lax.all_to_all(grad_first, "seq", split_axis=0, concat_axis=1, tiled=True)
    grad_tokens = jnp.einsum(
        "acb,acd->abd", block_one, arrived, preferred_element_type=jnp.float32
    ).astype(jnp.bfloat16)
    grad_block_one = (
        outer_one + jnp.einsum("acd,abd->acb", arrived, tokens, preferred_element_type=jnp.float32)
    ) * grad_scale
    grad_block_one, grad_block_two, grad_kernel = (
        lax.psum_scatter(grad_block_one, "dp", scatter_dimension=2, tiled=True),
        lax.psum_scatter(grad_block_two, "dp", scatter_dimension=2, tiled=True),
        lax.psum_scatter(grad_kernel, "dp", scatter_dimension=2, tiled=True),
    )
    return (
        output[None],
        grad_tokens[None],
        grad_gate[None],
        grad_kernel.astype(jnp.bfloat16),
        grad_block_one.astype(jnp.bfloat16),
        grad_block_two.astype(jnp.bfloat16),
    )


def solution(mesh):
    return jax.shard_map(
        body,
        mesh=mesh,
        in_specs=(
            P("dp", "seq", None, None),
            P("dp", "seq", None, None),
            P(None, "seq", None),
            P("dp", "seq", None, None),
            P("seq", None, None),
            P("seq", None, None),
        ),
        out_specs=(
            P("dp", "seq", None, None),
            P("dp", "seq", None, None),
            P("dp", "seq", None, None),
            P(None, "seq", "dp"),
            P("seq", None, "dp"),
            P("seq", None, "dp"),
        ),
        check_vma=False,
    )
```

profile of v0, /device:TPU:0, one launch (start us, length us, event | category | flops | bytes accessed | tf_op | source)
XLA Modules:
  0.0 1188.4 jit_solution(1900922170163310603)
XLA Ops:
  31.7 12.7 %convert_bitcast_fusion.2 = bf16[16,512,512]{1,2,0:T(8,128)(2,1)} fusion(bf16[16,512,512]{2,1,0:T(8,128)(2,1)} %param.10, bf16[1,16,512,512]{2,3,1,0:T(8,128)(2,1)} %copy.86, bf16[1,16,512,512]{2,3,1,0:T(8,128)(2,1)} %copy.77), kind=kOutput, calls=%fused_computation.25 | convolution fusion | flops 4328521728 | bytes 33554432 | tf_op jit(solution)/shard_map/fch,fhd->fcd/dot_general | solution.py:35
  44.4 14.9 %copy.87 = bf16[16,512,512]{2,0,1:T(8,128)(2,1)} copy(bf16[16,512,512]{1,2,0:T(8,128)(2,1)} %convert_bitcast_fusion.2) | data formatting | bytes 16777216 | tf_op jit(solution)/shard_map/convert_element_type | solution.py:37
  66.9 13.7 %fusion.21 = bf16[16,512,512]{2,1,0:T(8,128)(2,1)} fusion(bf16[16,512,512]{2,1,0:T(8,128)(2,1)} %param.10, bf16[1,16,512,512]{3,2,1,0:T(8,128)(2,1)} %param.6), kind=kOutput, calls=%fused_computation.35 | convolution fusion | flops 4299161600 | bytes 25165824 | tf_op jit(solution)/shard_map/acb,abd->acd/dot_general | solution.py:11
  91.9 125.5 %all-to-all-done.2 = bf16[16,512,512]{2,0,1:T(8,128)(2,1)} async-done(((bf16[16,512,512]{2,0,1:T(8,128)(2,1)}), bf16[16,512,512]{2,0,1:T(8,128)(2,1)}, u32[]{:S(2)}, u32[]{:S(2)}) %all-to-all-start.2) | async-done | bytes 8388640 | tf_op jit(solution)/shard_map/all_to_all | solution.py:38
  217.5 36.5 %all-to-all-start = ((bf16[16,512,512]{2,0,1:T(8,128)(2,1)}), bf16[16,512,512]{2,0,1:T(8,128)(2,1)}, u32[]{:S(2)}, u32[]{:S(2)}) async-start(bf16[16,512,512]{2,0,1:T(8,128)(2,1)} %copy.79), calls=%async_computation | async-start | bytes 16777216 | tf_op jit(solution)/shard_map/all_to_all | solution.py:14
  254.0 13.9 %copy.78 = bf16[256,32,512]{0,2,1:T(8,128)(2,1)} copy(bf16[256,32,512]{2,1,0:T(8,128)(2,1)} %param.8) | data formatting | bytes 16777216 | tf_op args[2]
  280.2 124.3 %all-to-all-done = bf16[16,512,512]{2,0,1:T(8,128)(2,1)} async-done(((bf16[16,512,512]{2,0,1:T(8,128)(2,1)}), bf16[16,512,512]{2,0,1:T(8,128)(2,1)}, u32[]{:S(2)}, u32[]{:S(2)}) %all-to-all-start) | async-done | bytes 8388640 | tf_op jit(solution)/shard_map/all_to_all | solution.py:14
  404.6 12.7 %copy.81 = bf16[16,16,32,512]{3,2,1,0:T(8,128)(2,1)} copy(bf16[16,16,32,512]{3,1,2,0:T(8,128)(2,1)} %bitcast.4) | data formatting | bytes 16777216 | tf_op jit(solution)/shard_map/all_to_all | solution.py:14
  417.3 20.4 %fusion.13 = f32[32,512,256]{2,1,0:T(8,128)} fusion(bf16[32,256,256]{2,1,0:T(8,128)(2,1)} %param.11, bf16[256,32,512]{2,1,0:T(8,128)(2,1)} %bitcast.89), kind=kOutput, calls=%fused_computation.27 | convolution fusion | flops 2147483648 | bytes 29360128 | tf_op jit(solution)/shard_map/cea,acd->ecd/dot_general | solution.py:16
  437.6 22.1 %bitcast_multiply_fusion = (f32[256,32,512]{0,2,1:T(8,128)}, f32[32,512,256]{2,1,0:T(8,128)}) fusion(f32[32,512,256]{2,1,0:T(8,128)} %fusion.13, bf16[32,256,256]{2,1,0:T(8,128)(2,1)} %param.11, bf16[256,32,512]{2,1,0:T(8,128)(2,1)} %bitcast.87), kind=kOutput, calls=%fused_computation.10 | convolution fusion | flops 2151677952 | bytes 62914560 | tf_op jit(solution)/shard_map/cef,fcd->ecd/dot_general | solution.py:40
  459.7 21.2 %fusion.15 = f32[32,256,256]{2,1,0:T(8,128)} fusion(bf16[256,32,512]{2,1,0:T(8,128)(2,1)} %bitcast.90, bf16[256,32,512]{0,2,1:T(8,128)(2,1)} %copy.78, f32[32,512,256]{2,1,0:T(8,128)} %get-tuple-element.33), kind=kOutput, calls=%fused_computation.29 | convolution fusion | flops 2160066560 | bytes 41943040 | tf_op jit(solution)/shard_map/ecd,acd->cea/dot_general | solution.py:50
  481.0 23.3 %add_multiply_fusion.1 = f32[32,256,256]{2,1,0:T(8,128)} fusion(f32[32,256,256]{2,1,0:T(8,128)} %fusion.15, bf16[256,32,512]{2,1,0:T(8,128)(2,1)} %bitcast.88, bf16[256,32,512]{0,2,1:T(8,128)(2,1)} %copy.78, f32[32,512,256]{2,1,0:T(8,128)} %fusion.13), kind=kOutput, calls=%fused_computation.22 | convolution fusion | flops 2164260864 | bytes 50331648 | tf_op jit(solution)/shard_map/fcd,ecd->cef/dot_general | solution.py:43
  504.3 14.2 %convert_bitcast_fusion.3 = bf16[256,32,512]{0,2,1:T(8,128)(2,1)} fusion(bf16[32,256,256]{2,1,0:T(8,128)(2,1)} %param.11, bf16[256,32,512]{0,2,1:T(8,128)(2,1)} %copy.78, f32[32,512,256]{2,1,0:T(8,128)} %fusion.13), kind=kOutput, calls=%fused_computation.26 | convolution fusion | flops 2164260864 | bytes 37748736 | tf_op jit(solution)/shard_map/cef,ecd->fcd/dot_general | solution.py:18
  518.5 14.6 %copy.83 = bf16[256,32,512]{2,1,0:T(8,128)(2,1)} copy(bf16[256,32,512]{0,2,1:T(8,128)(2,1)} %convert_bitcast_fusion.3) | data formatting | bytes 16777216 | tf_op jit(solution)/shard_map/convert_element_type | solution.py:20
  533.2 37.2 %all-to-all-start.1 = ((bf16[256,32,512]{2,1,0:T(8,128)(2,1)}), bf16[256,32,512]{2,1,0:T(8,128)(2,1)}, u32[]{:S(2)}, u32[]{:S(2)}) async-start(bf16[256,32,512]{2,1,0:T(8,128)(2,1)} %copy.83), calls=%async_computation.1 | async-start | bytes 16777216 | tf_op jit(solution)/shard_map/all_to_all | solution.py:21
  571.1 14.6 %convert_bitcast_fusion.1 = bf16[256,32,512]{0,2,1:T(8,128)(2,1)} fusion(bf16[32,256,256]{2,1,0:T(8,128)(2,1)} %param.11, bf16[256,32,512]{0,2,1:T(8,128)(2,1)} %copy.78, f32[32,512,256]{2,1,0:T(8,128)} %get-tuple-element.33), kind=kOutput, calls=%fused_computation.24 | convolution fusion | flops 2164260864 | bytes 37748736 | tf_op jit(solution)/shard_map/cea,ecd->acd/dot_general | solution.py:52
  585.7 14.8 %copy.91 = bf16[256,32,512]{2,1,0:T(8,128)(2,1)} copy(bf16[256,32,512]{0,2,1:T(8,128)(2,1)} %convert_bitcast_fusion.1) | data formatting | bytes 16777216 | tf_op jit(solution)/shard_map/convert_element_type | solution.py:54
  600.5 120.5 %all-to-all-done.1 = bf16[256,32,512]{2,1,0:T(8,128)(2,1)} async-done(((bf16[256,32,512]{2,1,0:T(8,128)(2,1)}), bf16[256,32,512]{2,1,0:T(8,128)(2,1)}, u32[]{:S(2)}, u32[]{:S(2)}) %all-to-all-start.1) | async-done | bytes 8388640 | tf_op jit(solution)/shard_map/all_to_all | solution.py:21
  721.0 36.5 %all-to-all-start.3 = ((bf16[256,32,512]{2,1,0:T(8,128)(2,1)}), bf16[256,32,512]{2,1,0:T(8,128)(2,1)}, u32[]{:S(2)}, u32[]{:S(2)}) async-start(bf16[256,32,512]{2,1,0:T(8,128)(2,1)} %copy.91), calls=%async_computation.3 | async-start | bytes 16777216 | tf_op jit(solution)/shard_map/all_to_all | solution.py:55
  766.2 141.8 %all-to-all-done.3 = bf16[256,32,512]{2,1,0:T(8,128)(2,1)} async-done(((bf16[256,32,512]{2,1,0:T(8,128)(2,1)}), bf16[256,32,512]{2,1,0:T(8,128)(2,1)}, u32[]{:S(2)}, u32[]{:S(2)}) %all-to-all-start.3) | async-done | bytes 8388640 | tf_op jit(solution)/shard_map/all_to_all | solution.py:55
  916.3 16.1 %fusion.9 = f32[16,512,512]{2,1,0:T(8,128)} fusion(bf16[16,512,512]{2,1,0:T(8,128)(2,1)} %bitcast.91, bf16[1,16,512,512]{3,2,1,0:T(8,128)(2,1)} %param.6), kind=kOutput, calls=%fused_computation.18 | convolution fusion | flops 4294967296 | bytes 33554432 | tf_op jit(solution)/shard_map/acd,abd->acb/dot_general | solution.py:60
  932.4 22.1 %add_multiply_fusion = f32[16,512,512]{2,1,0:T(8,128)} fusion(f32[16,512,512]{2,1,0:T(8,128)} %fusion.9, bf16[16,512,512]{2,1,0:T(8,128)(2,1)} %bitcast.93, bf16[1,16,512,512]{2,3,1,0:T(8,128)(2,1)} %copy.86, bf16[1,16,512,512]{2,3,1,0:T(8,128)(2,1)} %copy.77), kind=kOutput, calls=%fused_computation.14 | convolution fusion | flops 4332716032 | bytes 58720256 | tf_op jit(solution)/shard_map/fhd,fcd->fch/dot_general | solution.py:32
  954.5 20.4 %fusion.8 = (bf16[1,16,512,512]{2,3,1,0:T(8,128)(2,1)}, bf16[1,16,512,512]{2,3,1,0:T(8,128)(2,1)}) fusion(bf16[1,16,512,512]{2,3,1,0:T(8,128)(2,1)} %copy.86, bf16[1,16,512,512]{2,3,1,0:T(8,128)(2,1)} %copy.77, bf16[16,512,512]{2,1,0:T(8,128)(2,1)} %bitcast.94, bf16[16,512,512]{2,1,0:T(8,128)(2,1)} %param.10), kind=kOutput, calls=%fused_computation.17 | convolution fusion | flops 4353687552 | bytes 50331648 | tf_op jit(solution)/shard_map/fch,fcd->fhd/dot_general | solution.py:23
  1041.4 134.3 %reduce-scatter.6.cloned.1.call-done = f32[16,512,256]{2,1,0:T(8,128)} async-done(((f32[16,512,512]{2,1,0:T(8,128)}), f32[16,512,256]{2,1,0:T(8,128)}) %reduce-scatter.6.cloned.1.call-update) | async-done | bytes 8388624 | tf_op jit(solution)/shard_map/reduce_scatter | solution.py:63
  (23 shorter events, 146.0 us)
Async XLA Ops:
  59.3 158.2 %all-to-all-start.2 = ((bf16[16,512,512]{2,0,1:T(8,128)(2,1)}), bf16[16,512,512]{2,0,1:T(8,128)(2,1)}, u32[]{:S(2)}, u32[]{:S(2)}) async-start(bf16[16,512,512]{2,0,1:T(8,128)(2,1)} %copy.87), calls=%async_computation.2 | async-start | bytes 16777216 | tf_op jit(solution)/shard_map/all_to_all | solution.py:38
  217.5 187.1 %all-to-all-start = ((bf16[16,512,512]{2,0,1:T(8,128)(2,1)}), bf16[16,512,512]{2,0,1:T(8,128)(2,1)}, u32[]{:S(2)}, u32[]{:S(2)}) async-start(bf16[16,512,512]{2,0,1:T(8,128)(2,1)} %copy.79), calls=%async_computation | async-start | bytes 16777216 | tf_op jit(solution)/shard_map/all_to_all | solution.py:14
  254.0 769.3 %reduce-scatter.8.cloned.1.call-start = ((), (), s32[]{:S(2)}) async-start(), calls=%async_computation.9 | async-start | bytes 12582912 | tf_op jit(solution)/shard_map/reduce_scatter | solution.py:64
  533.2 187.8 %all-to-all-start.1 = ((bf16[256,32,512]{2,1,0:T(8,128)(2,1)}), bf16[256,32,512]{2,1,0:T(8,128)(2,1)}, u32[]{:S(2)}, u32[]{:S(2)}) async-start(bf16[256,32,512]{2,1,0:T(8,128)(2,1)} %copy.83), calls=%async_computation.1 | async-start | bytes 16777216 | tf_op jit(solution)/shard_map/all_to_all | solution.py:21
  570.4 457.0 %reduce-scatter.4.cloned.1.call-start = ((), (), s32[]{:S(2)}) async-start(), calls=%async_computation.7 | async-start | bytes 25165824 | tf_op jit(solution)/shard_map/reduce_scatter | solution.py:65
  721.0 187.1 %all-to-all-start.3 = ((bf16[256,32,512]{2,1,0:T(8,128)(2,1)}), bf16[256,32,512]{2,1,0:T(8,128)(2,1)}, u32[]{:S(2)}, u32[]{:S(2)}) async-start(bf16[256,32,512]{2,1,0:T(8,128)(2,1)} %copy.91), calls=%async_computation.3 | async-start | bytes 16777216 | tf_op jit(solution)/shard_map/all_to_all | solution.py:55
  757.5 418.2 %reduce-scatter.6.cloned.1.call-start = ((), (), s32[]{:S(2)}) async-start(), calls=%async_computation.8 | async-start | bytes 25165824 | tf_op jit(solution)/shard_map/reduce_scatter | solution.py:63
Sparse Core Ops, SparseCore 0:
  504.4 131.1 reduce-scatter.7
  637.9 189.1 reduce-scatter.3
  954.6 221.0 reduce-scatter.5
where the time goes:
time: 1200 us; the launch traced here: 1190 us
  waiting for transfers between devices  647 us (54%)
  matrix products  212 us (18%)
  local copies, waits for them, and re-layouts  181 us (15%)
  starting transfers between devices  118 us (10%)
  other arithmetic  16.2 us (1%)
  between operations  14.1 us (1%)
    all_to_all x1, waiting for transfers between devices, body(): lax.all_to_all(grad_first, 'seq', split_axis=0, concat_axis=1, tiled=True)  142 us
    reduce_scatter x1, waiting for transfers between devices, body(): lax.psum_scatter(grad_block_one, 'dp', scatter_dimension=2, tiled=True)  134 us
    all_to_all x1, waiting for transfers between devices, body(): lax.all_to_all(grad_third, 'seq', split_axis=1, concat_axis=0, tiled=True)  126 us
    all_to_all x1, waiting for transfers between devices, body(): lax.all_to_all(first, 'seq', split_axis=1, concat_axis=0, tiled=True)  124 us
    all_to_all x1, waiting for transfers between devices, body(): lax.all_to_all(third, 'seq', split_axis=0, concat_axis=1, tiled=True)  120 us
    unnamed x7, local copies, waits for them, and re-layouts  83 us
    all_to_all x1, starting transfers between devices, body(): lax.all_to_all(third, 'seq', split_axis=0, concat_axis=1, tiled=True)  37.2 us
    all_to_all x1, starting transfers between devices, body(): lax.all_to_all(grad_first, 'seq', split_axis=0, concat_axis=1, tiled=True)  36.5 us
  transfers between devices with their start and end apart: 7, of which 5 were waited for; matrix products, arithmetic and copies ran while one was open for 21% of the time, Pallas kernels for 0%

commit v1 on v0

--- a/solution.py
+++ b/solution.py
@@ -35,7 +35,9 @@
     grad_third = jnp.einsum(
         "fch,fhd->fcd", block_one, grad_fourth, preferred_element_type=jnp.float32
     ).astype(jnp.bfloat16)
-    arrived = lax.all_to_all(grad_third, "seq", split_axis=1, concat_axis=0, tiled=True)
+    shards = jnp.split(grad_third, lax.axis_size("seq"), axis=1)
+    arrived_2 = lax.all_to_all(jnp.stack(shards), "seq", 0, 0)
+    arrived = jnp.concatenate(arrived_2, axis=0)
     grad_third_cols = arrived
     grad_filtered = jnp.einsum(
         "cef,fcd->ecd", block_two, arrived, preferred_element_type=jnp.float32

time: 1200 us -> 1140 us (0.950)
  waiting for transfers between devices: 647 us -> 572 us
  matrix products: 212 us -> 225 us
    all_to_all x1, waiting for transfers between devices: 124 us -> 82.8 us  [body(): lax.all_to_all(first, 'seq', split_axis=1, concat_axis=0, tiled=True)]
    all_to_all x1, waiting for transfers between devices: 126 us -> 91.6 us  [body(): arrived_2 = lax.all_to_all(jnp.stack(shards), 'seq', 0, 0)]
    all_to_all x1, starting transfers between devices: 7.62 us -> 36.5 us  [body(): arrived_2 = lax.all_to_all(jnp.stack(shards), 'seq', 0, 0)]
    all_to_all x1, starting transfers between devices: 36.5 us -> 7.71 us  [body(): lax.all_to_all(first, 'seq', split_axis=1, concat_axis=0, tiled=True)]
    unnamed x7 -> x22, local copies, waits for them, and re-layouts: 83 us -> 111 us
    all_to_all x1, waiting for transfers between devices: 120 us -> 142 us  [body(): lax.all_to_all(third, 'seq', split_axis=0, concat_axis=1, tiled=True)]
    all_to_all x1, waiting for transfers between devices: 142 us -> 121 us  [body(): lax.all_to_all(grad_first, 'seq', split_axis=0, concat_axis=1, tiled=True)]
    convert_element_type x1 -> x0, local copies, waits for them, and re-layouts: 14.9 us -> none  [body(): grad_third = jnp.einsum('fch,fhd->fcd', block_one, grad_fourth, preferred...]
  transfers between devices with their start and end apart: 7 -> 7, of which waited for: 5 -> 5; matrix products, arithmetic and copies ran while one was open for 21% -> 29% of each run, Pallas kernels for 0% -> 0%
where the time goes in v1:
time: 1140 us; the launch traced here: 1130 us
  waiting for transfers between devices  572 us (50%)
  matrix products  225 us (20%)
  local copies, waits for them, and re-layouts  183 us (16%)
  starting transfers between devices  118 us (10%)
  other arithmetic  16.2 us (1%)
  between operations  14.2 us (1%)
    all_to_all x1, waiting for transfers between devices, body(): lax.all_to_all(third, 'seq', split_axis=0, concat_axis=1, tiled=True)  142 us
    reduce_scatter x1, waiting for transfers between devices, body(): lax.psum_scatter(grad_block_one, 'dp', scatter_dimension=2, tiled=True)  134 us
    all_to_all x1, waiting for transfers between devices, body(): lax.all_to_all(grad_first, 'seq', split_axis=0, concat_axis=1, tiled=True)  121 us
    unnamed x22, local copies, waits for them, and re-layouts  111 us
    all_to_all x1, waiting for transfers between devices, body(): arrived_2 = lax.all_to_all(jnp.stack(shards), 'seq', 0, 0)  91.6 us
    all_to_all x1, waiting for transfers between devices, body(): lax.all_to_all(first, 'seq', split_axis=1, concat_axis=0, tiled=True)  82.8 us
    all_to_all x1, starting transfers between devices, body(): lax.all_to_all(grad_first, 'seq', split_axis=0, concat_axis=1, tiled=True)  37.2 us
    all_to_all x1, starting transfers between devices, body(): lax.all_to_all(third, 'seq', split_axis=0, concat_axis=1, tiled=True)  36.5 us
  transfers between devices with their start and end apart: 7, of which 5 were waited for; matrix products, arithmetic and copies ran while one was open for 29% of the time, Pallas kernels for 0%

profile of v1, /device:TPU:0, one launch (start us, length us, event | category | flops | bytes accessed | tf_op | source)
XLA Modules:
  0.0 1128.6 jit_solution(11655630146661990161)
XLA Ops:
  7.2 13.7 %fusion.21 = bf16[16,512,512]{2,1,0:T(8,128)(2,1)} fusion(bf16[16,512,512]{2,1,0:T(8,128)(2,1)} %param.10, bf16[1,16,512,512]{3,2,1,0:T(8,128)(2,1)} %param.6), kind=kOutput, calls=%fused_computation.35 | convolution fusion | flops 4299161600 | bytes 25165824 | tf_op jit(solution)/shard_map/acb,abd->acd/dot_general | solution.py:11
  64.6 12.9 %convert_bitcast_fusion.2 = bf16[16,512,512]{2,1,0:T(8,128)(2,1)} fusion(bf16[16,512,512]{2,1,0:T(8,128)(2,1)} %param.10, bf16[1,16,512,512]{2,3,1,0:T(8,128)(2,1)} %copy.84, bf16[1,16,512,512]{2,3,1,0:T(8,128)(2,1)} %copy.75), kind=kOutput, calls=%fused_computation.25 | convolution fusion | flops 4328521728 | bytes 33554432 | tf_op jit(solution)/shard_map/fch,fhd->fcd/dot_general | solution.py:35
  107.9 82.8 %all-to-all-done = bf16[16,512,512]{2,0,1:T(8,128)(2,1)} async-done(((bf16[16,512,512]{2,0,1:T(8,128)(2,1)}), bf16[16,512,512]{2,0,1:T(8,128)(2,1)}, u32[]{:S(2)}, u32[]{:S(2)}) %all-to-all-start) | async-done | bytes 8388640 | tf_op jit(solution)/shard_map/all_to_all | solution.py:14
  190.6 36.5 %all-to-all-start.2 = ((bf16[16,16,32,512]{3,2,1,0:T(8,128)(2,1)}), bf16[16,16,32,512]{3,2,1,0:T(8,128)(2,1)}, u32[]{:S(2)}, u32[]{:S(2)}) async-start(bf16[16,16,32,512]{3,2,1,0:T(8,128)(2,1)} %fusion.26), calls=%async_computation.2 | async-start | bytes 16777216 | tf_op jit(solution)/shard_map/all_to_all | solution.py:39
  227.2 13.7 %copy.76 = bf16[256,32,512]{0,2,1:T(8,128)(2,1)} copy(bf16[256,32,512]{2,1,0:T(8,128)(2,1)} %param.8) | data formatting | bytes 16777216 | tf_op args[2]
  240.9 12.3 %copy.79 = bf16[16,16,32,512]{3,2,1,0:T(8,128)(2,1)} copy(bf16[16,16,32,512]{3,1,2,0:T(8,128)(2,1)} %bitcast.4) | data formatting | bytes 16777216 | tf_op jit(solution)/shard_map/all_to_all | solution.py:14
  253.2 32.9 %fusion.13 = f32[32,512,256]{2,1,0:T(8,128)} fusion(bf16[32,256,256]{2,1,0:T(8,128)(2,1)} %param.11, bf16[256,32,512]{2,1,0:T(8,128)(2,1)} %bitcast.148), kind=kOutput, calls=%fused_computation.27 | convolution fusion | flops 2147483648 | bytes 29360128 | tf_op jit(solution)/shard_map/cea,acd->ecd/dot_general | solution.py:16
  286.1 91.6 %all-to-all-done.2 = bf16[16,16,32,512]{3,2,1,0:T(8,128)(2,1)} async-done(((bf16[16,16,32,512]{3,2,1,0:T(8,128)(2,1)}), bf16[16,16,32,512]{3,2,1,0:T(8,128)(2,1)}, u32[]{:S(2)}, u32[]{:S(2)}) %all-to-all-start.2) | async-done | bytes 8388640 | tf_op jit(solution)/shard_map/all_to_all | solution.py:39
  377.8 21.9 %bitcast_multiply_fusion = (f32[256,32,512]{0,2,1:T(8,128)}, f32[32,512,256]{2,1,0:T(8,128)}) fusion(f32[32,512,256]{2,1,0:T(8,128)} %fusion.13, bf16[32,256,256]{2,1,0:T(8,128)(2,1)} %param.11, bf16[256,32,512]{2,1,0:T(8,128)(2,1)} %bitcast.31), kind=kOutput, calls=%fused_computation.10 | convolution fusion | flops 2151677952 | bytes 62914560 | tf_op jit(solution)/shard_map/cef,fcd->ecd/dot_general | solution.py:42
  399.7 21.3 %fusion.15 = f32[32,256,256]{2,1,0:T(8,128)} fusion(bf16[256,32,512]{2,1,0:T(8,128)(2,1)} %bitcast.149, bf16[256,32,512]{0,2,1:T(8,128)(2,1)} %copy.76, f32[32,512,256]{2,1,0:T(8,128)} %get-tuple-element.33), kind=kOutput, calls=%fused_computation.29 | convolution fusion | flops 2160066560 | bytes 41943040 | tf_op jit(solution)/shard_map/ecd,acd->cea/dot_general | solution.py:52
  421.0 23.1 %add_multiply_fusion.1 = f32[32,256,256]{2,1,0:T(8,128)} fusion(f32[32,256,256]{2,1,0:T(8,128)} %fusion.15, bf16[256,32,512]{2,1,0:T(8,128)(2,1)} %bitcast.31, bf16[256,32,512]{0,2,1:T(8,128)(2,1)} %copy.76, f32[32,512,256]{2,1,0:T(8,128)} %fusion.13), kind=kOutput, calls=%fused_computation.22 | convolution fusion | flops 2164260864 | bytes 50331648 | tf_op jit(solution)/shard_map/fcd,ecd->cef/dot_general | solution.py:45
  444.1 14.2 %convert_bitcast_fusion.1 = bf16[256,32,512]{0,2,1:T(8,128)(2,1)} fusion(bf16[32,256,256]{2,1,0:T(8,128)(2,1)} %param.11, bf16[256,32,512]{0,2,1:T(8,128)(2,1)} %copy.76, f32[32,512,256]{2,1,0:T(8,128)} %get-tuple-element.33), kind=kOutput, calls=%fused_computation.24 | convolution fusion | flops 2164260864 | bytes 37748736 | tf_op jit(solution)/shard_map/cea,ecd->acd/dot_general | solution.py:54
  458.3 14.8 %copy.87 = bf16[256,32,512]{2,1,0:T(8,128)(2,1)} copy(bf16[256,32,512]{0,2,1:T(8,128)(2,1)} %convert_bitcast_fusion.1) | data formatting | bytes 16777216 | tf_op jit(solution)/shard_map/convert_element_type | solution.py:56
  473.1 37.2 %all-to-all-start.3 = ((bf16[256,32,512]{2,1,0:T(8,128)(2,1)}), bf16[256,32,512]{2,1,0:T(8,128)(2,1)}, u32[]{:S(2)}, u32[]{:S(2)}) async-start(bf16[256,32,512]{2,1,0:T(8,128)(2,1)} %copy.87), calls=%async_computation.3 | async-start | bytes 16777216 | tf_op jit(solution)/shard_map/all_to_all | solution.py:57
  511.2 14.6 %convert_bitcast_fusion.3 = bf16[256,32,512]{0,2,1:T(8,128)(2,1)} fusion(bf16[32,256,256]{2,1,0:T(8,128)(2,1)} %param.11, bf16[256,32,512]{0,2,1:T(8,128)(2,1)} %copy.76, f32[32,512,256]{2,1,0:T(8,128)} %fusion.13), kind=kOutput, calls=%fused_computation.26 | convolution fusion | flops 2164260864 | bytes 37748736 | tf_op jit(solution)/shard_map/cef,ecd->fcd/dot_general | solution.py:18
  525.7 14.6 %copy.81 = bf16[256,32,512]{2,1,0:T(8,128)(2,1)} copy(bf16[256,32,512]{0,2,1:T(8,128)(2,1)} %convert_bitcast_fusion.3) | data formatting | bytes 16777216 | tf_op jit(solution)/shard_map/convert_element_type | solution.py:20
  540.4 120.6 %all-to-all-done.3 = bf16[256,32,512]{2,1,0:T(8,128)(2,1)} async-done(((bf16[256,32,512]{2,1,0:T(8,128)(2,1)}), bf16[256,32,512]{2,1,0:T(8,128)(2,1)}, u32[]{:S(2)}, u32[]{:S(2)}) %all-to-all-start.3) | async-done | bytes 8388640 | tf_op jit(solution)/shard_map/all_to_all | solution.py:57
  661.0 36.5 %all-to-all-start.1 = ((bf16[256,32,512]{2,1,0:T(8,128)(2,1)}), bf16[256,32,512]{2,1,0:T(8,128)(2,1)}, u32[]{:S(2)}, u32[]{:S(2)}) async-start(bf16[256,32,512]{2,1,0:T(8,128)(2,1)} %copy.81), calls=%async_computation.1 | async-start | bytes 16777216 | tf_op jit(solution)/shard_map/all_to_all | solution.py:21
  706.1 142.0 %all-to-all-done.1 = bf16[256,32,512]{2,1,0:T(8,128)(2,1)} async-done(((bf16[256,32,512]{2,1,0:T(8,128)(2,1)}), bf16[256,32,512]{2,1,0:T(8,128)(2,1)}, u32[]{:S(2)}, u32[]{:S(2)}) %all-to-all-start.1) | async-done | bytes 8388640 | tf_op jit(solution)/shard_map/all_to_all | solution.py:21
  856.4 16.1 %fusion.9 = f32[16,512,512]{2,1,0:T(8,128)} fusion(bf16[16,512,512]{2,1,0:T(8,128)(2,1)} %bitcast.150, bf16[1,16,512,512]{3,2,1,0:T(8,128)(2,1)} %param.6), kind=kOutput, calls=%fused_computation.18 | convolution fusion | flops 4294967296 | bytes 33554432 | tf_op jit(solution)/shard_map/acd,abd->acb/dot_general | solution.py:62
  872.4 22.1 %add_multiply_fusion = f32[16,512,512]{2,1,0:T(8,128)} fusion(f32[16,512,512]{2,1,0:T(8,128)} %fusion.9, bf16[16,512,512]{2,1,0:T(8,128)(2,1)} %bitcast.152, bf16[1,16,512,512]{2,3,1,0:T(8,128)(2,1)} %copy.84, bf16[1,16,512,512]{2,3,1,0:T(8,128)(2,1)} %copy.75), kind=kOutput, calls=%fused_computation.14 | convolution fusion | flops 4332716032 | bytes 58720256 | tf_op jit(solution)/shard_map/fhd,fcd->fch/dot_general | solution.py:32
  918.2 20.7 %fusion.8 = (bf16[1,16,512,512]{2,3,1,0:T(8,128)(2,1)}, bf16[1,16,512,512]{2,3,1,0:T(8,128)(2,1)}) fusion(bf16[1,16,512,512]{2,3,1,0:T(8,128)(2,1)} %copy.84, bf16[1,16,512,512]{2,3,1,0:T(8,128)(2,1)} %copy.75, bf16[16,512,512]{2,1,0:T(8,128)(2,1)} %bitcast.153, bf16[16,512,512]{2,1,0:T(8,128)(2,1)} %param.10), kind=kOutput, calls=%fused_computation.17 | convolution fusion | flops 4353687552 | bytes 50331648 | tf_op jit(solution)/shard_map/fch,fcd->fhd/dot_general | solution.py:23
  938.8 12.3 %copy.95 = bf16[1,16,512,512]{3,2,1,0:T(8,128)(2,1)} copy(bf16[1,16,512,512]{2,3,1,0:T(8,128)(2,1)} %get-tuple-element.31) | data formatting | bytes 16777216
  981.6 134.1 %reduce-scatter.6.cloned.1.call-done = f32[16,512,256]{2,1,0:T(8,128)} async-done(((f32[16,512,512]{2,1,0:T(8,128)}), f32[16,512,256]{2,1,0:T(8,128)}) %reduce-scatter.6.cloned.1.call-update) | async-done | bytes 8388624 | tf_op jit(solution)/shard_map/reduce_scatter | solution.py:65
  (37 shorter events, 151.7 us)
Async XLA Ops:
  32.4 158.3 %all-to-all-start = ((bf16[16,512,512]{2,0,1:T(8,128)(2,1)}), bf16[16,512,512]{2,0,1:T(8,128)(2,1)}, u32[]{:S(2)}, u32[]{:S(2)}) async-start(bf16[16,512,512]{2,0,1:T(8,128)(2,1)} %copy.77), calls=%async_computation | async-start | bytes 16777216 | tf_op jit(solution)/shard_map/all_to_all | solution.py:14
  190.6 187.1 %all-to-all-start.2 = ((bf16[16,16,32,512]{3,2,1,0:T(8,128)(2,1)}), bf16[16,16,32,512]{3,2,1,0:T(8,128)(2,1)}, u32[]{:S(2)}, u32[]{:S(2)}) async-start(bf16[16,16,32,512]{3,2,1,0:T(8,128)(2,1)} %fusion.26), calls=%async_computation.2 | async-start | bytes 16777216 | tf_op jit(solution)/shard_map/all_to_all | solution.py:39
  227.2 736.3 %reduce-scatter.8.cloned.1.call-start = ((), (), s32[]{:S(2)}) async-start(), calls=%async_computation.9 | async-start | bytes 12582912 | tf_op jit(solution)/shard_map/reduce_scatter | solution.py:66
  473.1 187.8 %all-to-all-start.3 = ((bf16[256,32,512]{2,1,0:T(8,128)(2,1)}), bf16[256,32,512]{2,1,0:T(8,128)(2,1)}, u32[]{:S(2)}, u32[]{:S(2)}) async-start(bf16[256,32,512]{2,1,0:T(8,128)(2,1)} %copy.87), calls=%async_computation.3 | async-start | bytes 16777216 | tf_op jit(solution)/shard_map/all_to_all | solution.py:57
  510.4 457.2 %reduce-scatter.4.cloned.1.call-start = ((), (), s32[]{:S(2)}) async-start(), calls=%async_computation.7 | async-start | bytes 25165824 | tf_op jit(solution)/shard_map/reduce_scatter | solution.py:67
  661.0 187.1 %all-to-all-start.1 = ((bf16[256,32,512]{2,1,0:T(8,128)(2,1)}), bf16[256,32,512]{2,1,0:T(8,128)(2,1)}, u32[]{:S(2)}, u32[]{:S(2)}) async-start(bf16[256,32,512]{2,1,0:T(8,128)(2,1)} %copy.81), calls=%async_computation.1 | async-start | bytes 16777216 | tf_op jit(solution)/shard_map/all_to_all | solution.py:21
  697.5 418.2 %reduce-scatter.6.cloned.1.call-start = ((), (), s32[]{:S(2)}) async-start(), calls=%async_computation.8 | async-start | bytes 25165824 | tf_op jit(solution)/shard_map/reduce_scatter | solution.py:65
Sparse Core Ops, SparseCore 0:
  444.2 131.1 reduce-scatter.7
  577.7 189.1 reduce-scatter.3
  894.6 220.9 reduce-scatter.5
